TPU v7x, 128 devices: a whole 4x4x4 slice. The times are simulated.
128 devices in a mesh: ctx: 16 (over y, x), grp: 8 (over z, core).
Axes of the slice: x: 4, y: 4, z: 4, core: 2. Of those that a mesh axis runs over, the one named last changes fastest.
Arguments:
- residual: bfloat16 [8, 2048, 2880], P('grp', 'ctx'), may hold values from -3 to 3
- queries: bfloat16 [8, 2048, 2048], P('grp', 'ctx'), may hold values from -8 to 8
- stretch_kv: bfloat16 [8, 2048, 1024], P('grp', 'ctx'), may hold values from -8 to 8
- cache_kv: bfloat16 [8, 4096, 1024], P('grp', 'ctx'), may hold values from -6 to 6
- doc_lengths: int32 [8, 8], P('grp'), may hold values from 1 to 3072, 6144 in all within a row
- sinks: float32 [32], replicated, may hold values from 2 to 6
- out_proj: bfloat16 [2048, 2880], P('ctx'), may hold values from -0.75 to 0.75
- norm_gain: float32 [2880], replicated, may hold values from 0.1 to 1.9
- router: bfloat16 [2880, 64], replicated, may hold values from -0.109375 to 0.109375
- expert_ids: int32 [8, 2048, 4], P('grp', 'ctx'), may hold values from 0 to 63, all different within a row; in each aligned block of 128 rows (0 to 127, 128 to 255, ..., all dimensions but the last counted through in order) at most 10 rows name the same one
- expert_in: bfloat16 [128, 2880, 1536], P(('ctx', 'grp')), may hold values from -0.109375 to 0.109375
- expert_out: bfloat16 [128, 768, 2880], P(('ctx', 'grp')), may hold values from -0.15625 to 0.15625
Outputs:
- resid_mid: bfloat16 [8, 2048, 2880], P('grp', 'ctx')
- layer_out: bfloat16 [8, 2048, 2880], P('grp', 'ctx')
Inputs may be any that keep to these rules, and one draw needn't show every extreme that they name: `expert_ids`: in the rows of one device (aligned blocks of 128 tokens, sequence after sequence), each expert is named by at most 10 rows, and in some blocks one expert by exactly 10; a token's 4 experts differ. `doc_lengths`: A sequence's 8 lengths sum to 6144; the longest is exactly 3072.
All inputs are finite; a program needn't handle non-finite values.
Results may differ from a plain program's by a relative error of at most 0.015.
Values may be sent and summed in bfloat16 or wider, within the bound.
No kernel may reach another device: no remote copies, remote signals or barrier semaphores. Data moves between devices by JAX's collectives and lax.ppermute only.
A program may use at most 128 MiB of HBM per device.

v0:
```python
import math
import jax
import jax.numpy as jnp
from jax import lax
from jax.sharding import PartitionSpec as P

HEADS = 32
KVH = 8
HD = 64


def doc_index(positions, lengths):
    ends = jnp.cumsum(lengths)
    return jnp.sum((positions[:, None] >= ends[None, :]).astype(jnp.int32), axis=1)


def gated_act(pre, half_width):
    gate = pre[:, :half_width]
    upper = pre[:, half_width:]
    return ((upper + 1.0) * gate * jax.nn.sigmoid(1.702 * gate)).astype(jnp.bfloat16)


def body(
    residual,
    queries,
    stretch_kv,
    cache_kv,
    doc_lengths,
    sinks,
    out_proj,
    norm_gain,
    router,
    expert_ids,
    expert_in,
    expert_out,
):
    tokens = residual.shape[1]
    width = residual.shape[2]
    cache_rows = cache_kv.shape[1]
    kv_cols = stretch_kv.shape[2] // 2
    groups = HEADS // KVH
    ctx_count = lax.axis_size("ctx")
    ctx_here = lax.axis_index("ctx")
    stretch_base = cache_rows * ctx_count
    span = cache_rows + tokens
    query_pos = stretch_base + ctx_here * tokens + jnp.arange(tokens, dtype=jnp.int32)
    lengths = doc_lengths[0]
    query_doc = doc_index(query_pos, lengths)
    query_heads = queries[0].reshape(tokens, KVH, groups, HD)
    sink_grid = sinks.reshape(KVH, groups)
    local_kv = jnp.concatenate([cache_kv[0], stretch_kv[0]], axis=0)
    scale = 1.0 / math.sqrt(HD)

    def key_block(carry, keys_values, first):
        count = keys_values.shape[0]
        rows = first + jnp.arange(count, dtype=jnp.int32)
        source = rows // span
        offset = rows % span
        key_pos = jnp.where(
            offset < cache_rows,
            source * cache_rows + offset,
            stretch_base + source * tokens + offset - cache_rows,
        )
        key_doc = doc_index(key_pos, lengths)
        allowed = (key_pos[None, :] <= query_pos[:, None]) & (
            key_doc[None, :] == query_doc[:, None]
        )
        keys = keys_values[:, :kv_cols].reshape(count, KVH, HD)
        values = keys_values[:, kv_cols:].reshape(count, KVH, HD)
        top, total, numer = carry
        scores = (
            jnp.einsum("qkgd,skd->kgqs", query_heads, keys, preferred_element_type=jnp.float32)
            * scale
        )
        masked = jnp.where(allowed[None, None], scores, -jnp.inf)
        new_top = jnp.maximum(top, jnp.max(masked, axis=-1))
        weights = jnp.where(allowed[None, None], jnp.exp(scores - new_top[..., None]), 0.0)
        shrink = jnp.exp(top - new_top)
        total = total * shrink + jnp.sum(weights, axis=-1)
        numer = numer * shrink[..., None] + jnp.einsum(
            "kgqs,skd->kgqd",
            weights.astype(jnp.bfloat16),
            values,
            preferred_element_type=jnp.float32,
        )
        return (new_top, total, numer)

    start_top = jnp.broadcast_to(sink_grid[:, :, None], (KVH, groups, tokens))
    start_total = jnp.zeros((KVH, groups, tokens), jnp.float32)
    start_numer = jnp.zeros((KVH, groups, tokens, HD), jnp.float32)
    piece = lax.all_gather(local_kv, "ctx", axis=0, tiled=True)
    count = piece.shape[0]
    step_rows = math.gcd(count, 1024)

    def advance(index, state):
        first = index * step_rows
        part = lax.dynamic_slice_in_dim(piece, first, step_rows, 0)
        return key_block(state, part, first)

    top, total, numer = lax.fori_loop(
        0, count // step_rows, advance, (start_top, start_total, start_numer)
    )
    denom = total + jnp.exp(sink_grid[:, :, None] - top)
    attended = (
        jnp.transpose(numer / denom[..., None], (2, 0, 1, 3))
        .reshape(tokens, HEADS * HD)
        .astype(jnp.bfloat16)
    )
    projected = jnp.dot(
        attended,
        lax.all_gather(out_proj, "ctx", axis=0, tiled=True),
        preferred_element_type=jnp.float32,
    )
    mid = (residual[0].astype(jnp.float32) + projected).astype(jnp.bfloat16)
    mid_float = mid.astype(jnp.float32)
    normed = (
        mid_float
        * lax.rsqrt(jnp.mean(mid_float * mid_float, axis=-1, keepdims=True) + 1e-05)
        * norm_gain
    ).astype(jnp.bfloat16)
    logits = jnp.dot(normed, router, preferred_element_type=jnp.float32)
    experts = router.shape[1]
    chosen_ids = expert_ids[0]
    topk = chosen_ids.shape[1]
    picks = chosen_ids[:, :, None] == jnp.arange(experts, dtype=jnp.int32)[None, None, :]
    chosen = jnp.sum(jnp.where(picks, logits[:, None, :], 0.0), axis=-1)
    raised = jnp.exp(chosen)
    route_weights = raised / jnp.sum(raised, axis=-1, keepdims=True)
    capacity = 2 * ((5 * tokens * topk + 8 * experts - 1) // (8 * experts))
    flat_ids = chosen_ids.reshape(-1)
    pairs = flat_ids.shape[0]
    onehot = (flat_ids[:, None] == jnp.arange(experts, dtype=jnp.int32)[None, :]).astype(jnp.int32)
    slots = jnp.sum(onehot * (jnp.cumsum(onehot, axis=0) - 1), axis=1)
    dest = flat_ids * capacity + slots
    source_rows = jnp.arange(pairs, dtype=jnp.int32) // topk
    packed = jnp.zeros((experts * capacity, width), jnp.bfloat16).at[dest].set(normed[source_rows])
    packed = packed.reshape(experts, capacity, width)
    in_weights = expert_in[0]
    out_weights = expert_out[0]
    half_width = out_weights.shape[0]
    doubled = jnp.broadcast_to(packed[:, None], (experts, 2, capacity, width)).reshape(
        2 * experts, capacity, width
    )
    received = lax.all_to_all(doubled, ("ctx", "grp"), split_axis=0, concat_axis=0, tiled=True)
    flat_rows = received.reshape(-1, width)
    pre = jnp.dot(flat_rows, in_weights, preferred_element_type=jnp.float32)
    hidden = gated_act(pre, half_width)
    partial_out = jnp.dot(hidden, out_weights, preferred_element_type=jnp.float32).astype(
        jnp.bfloat16
    )
    partial_out = partial_out.reshape(received.shape)
    returned = lax.all_to_all(partial_out, ("ctx", "grp"), split_axis=0, concat_axis=0, tiled=True)
    pair_total = jnp.sum(returned.reshape(experts, 2, capacity, width).astype(jnp.float32), axis=1)
    expert_rows = pair_total.astype(jnp.bfloat16).reshape(experts * capacity, width)
    gathered = expert_rows[dest].astype(jnp.float32) * route_weights.reshape(-1)[:, None]
    mixture = jnp.sum(gathered.reshape(tokens, topk, width), axis=1)
    final = (mid_float + mixture).astype(jnp.bfloat16)
    return (mid[None], final[None])


def solution(mesh):
    return jax.shard_map(
        body,
        mesh=mesh,
        in_specs=(
            P("grp", "ctx", None),
            P("grp", "ctx", None),
            P("grp", "ctx", None),
            P("grp", "ctx", None),
            P("grp", None),
            P(),
            P("ctx", None),
            P(),
            P(),
            P("grp", "ctx", None),
            P(("ctx", "grp"), None, None),
            P(("ctx", "grp"), None, None),
        ),
        out_specs=(P("grp", "ctx", None), P("grp", "ctx", None)),
        check_vma=False,
    )
```

profile of v0, /device:TPU:66, one launch (start us, length us, event | category | flops | bytes accessed | tf_op | source)
XLA Modules:
  0.0 739.0 jit_solution(131095022201304216)
XLA Ops:
  14.6 97.2 %all-gather.3.cloned.1.call-done = bf16[6144,1024]{0,1:T(8,128)(2,1)} async-done(((bf16[384,1024]{0,1:T(8,128)(2,1)}), bf16[6144,1024]{0,1:T(8,128)(2,1)}) %all-gather.3.cloned.1.call-update) | async-done | bytes 12582928 | tf_op jit(solution)/shard_map/all_gather | solution.py:91
  111.8 157.7 %while.20 = (s32[]{:T(128)}, f32[8,4,128]{2,1,0:T(4,128)S(1)}, f32[8,4,128]{2,1,0:T(4,128)S(1)}, f32[8,4,128,64]{2,3,1,0:T(8,128)S(1)}, s32[1,8]{1,0:T(1,128)S(1...) while((s32[]{:T(128)}, f32[8,4,128]{2,1,0:T(4,128)S(1)}, ...), condition=%wide.region_7.8_spmd.clone, body=%wide.region_3.7_spmd.clone.sunk | while | flops 1121116288 | bytes 60053240 | solution.py:100
  114.0 7.1 fusion.69
  121.1 9.8 %fusion.70 = f32[8,4,128]{2,1,0:T(4,128)S(1)} fusion(f32[8,1024,128,4]{2,1,3,0:T(8,128)} %get-tuple-element.355, f32[8,4,128]{2,1,0:T(4,128)S(1)} %max.12, pred[128,1024]{0,1:T(8,128)(4,1)S(1)} %compare_and_fusion.2), kind=kLoop, calls=%fused_computation.10.clone.1 | loop fusion | flops 16773120 | bytes 16941056 | tf_op jit(solution)/shard_map/while/body/eval_jaxpr/reduce_sum | solution.py:79
  130.9 7.6 %fusion.72 = f32[8,4,128,64]{2,3,1,0:T(8,128)S(1)} fusion(bf16[1024,8,64,1]{0,2,3,1:T(8,128)(2,1)S(1)} %bitcast.98, f32[8,1024,128,4]{2,1,3,0:T(8,128)} %get-tuple-element.355, f32[8,4,128]{2,1,0:T(4,128)S(1)} %max.12, pred[128,1024]{0,1:T(8,128)(4,1)S(1)} %compare_and_fusion.2, f32[8,4,128,64]{2,3,1,0:T(8,128)S(1)} %get-tuple-element.376, ...), kind=kOutput, calls=%fused_computation.13.clone.1 | convolution fusion | flops 554434560 | bytes 20086784 | tf_op jit(solution)/shard_map/while/body/eval_jaxpr/kgqs,skd->kgqd/dot_general | solution.py:80
  140.9 7.1 fusion.69
  147.9 9.1 %fusion.70 = f32[8,4,128]{2,1,0:T(4,128)S(1)} fusion(f32[8,1024,128,4]{2,1,3,0:T(8,128)} %get-tuple-element.355, f32[8,4,128]{2,1,0:T(4,128)S(1)} %max.12, pred[128,1024]{0,1:T(8,128)(4,1)S(1)} %compare_and_fusion.2), kind=kLoop, calls=%fused_computation.10.clone.1 | loop fusion | flops 16773120 | bytes 16941056 | tf_op jit(solution)/shard_map/while/body/eval_jaxpr/reduce_sum | solution.py:79
  157.1 7.8 %fusion.72 = f32[8,4,128,64]{2,3,1,0:T(8,128)S(1)} fusion(bf16[1024,8,64,1]{0,2,3,1:T(8,128)(2,1)S(1)} %bitcast.98, f32[8,1024,128,4]{2,1,3,0:T(8,128)} %get-tuple-element.355, f32[8,4,128]{2,1,0:T(4,128)S(1)} %max.12, pred[128,1024]{0,1:T(8,128)(4,1)S(1)} %compare_and_fusion.2, f32[8,4,128,64]{2,3,1,0:T(8,128)S(1)} %get-tuple-element.376, ...), kind=kOutput, calls=%fused_computation.13.clone.1 | convolution fusion | flops 554434560 | bytes 20086784 | tf_op jit(solution)/shard_map/while/body/eval_jaxpr/kgqs,skd->kgqd/dot_general | solution.py:80
  167.1 7.2 fusion.69
  174.3 9.8 %fusion.70 = f32[8,4,128]{2,1,0:T(4,128)S(1)} fusion(f32[8,1024,128,4]{2,1,3,0:T(8,128)} %get-tuple-element.355, f32[8,4,128]{2,1,0:T(4,128)S(1)} %max.12, pred[128,1024]{0,1:T(8,128)(4,1)S(1)} %compare_and_fusion.2), kind=kLoop, calls=%fused_computation.10.clone.1 | loop fusion | flops 16773120 | bytes 16941056 | tf_op jit(solution)/shard_map/while/body/eval_jaxpr/reduce_sum | solution.py:79
  184.2 7.4 %fusion.72 = f32[8,4,128,64]{2,3,1,0:T(8,128)S(1)} fusion(bf16[1024,8,64,1]{0,2,3,1:T(8,128)(2,1)S(1)} %bitcast.98, f32[8,1024,128,4]{2,1,3,0:T(8,128)} %get-tuple-element.355, f32[8,4,128]{2,1,0:T(4,128)S(1)} %max.12, pred[128,1024]{0,1:T(8,128)(4,1)S(1)} %compare_and_fusion.2, f32[8,4,128,64]{2,3,1,0:T(8,128)S(1)} %get-tuple-element.376, ...), kind=kOutput, calls=%fused_computation.13.clone.1 | convolution fusion | flops 554434560 | bytes 20086784 | tf_op jit(solution)/shard_map/while/body/eval_jaxpr/kgqs,skd->kgqd/dot_general | solution.py:80
  193.9 7.2 fusion.69
  201.1 9.1 %fusion.70 = f32[8,4,128]{2,1,0:T(4,128)S(1)} fusion(f32[8,1024,128,4]{2,1,3,0:T(8,128)} %get-tuple-element.355, f32[8,4,128]{2,1,0:T(4,128)S(1)} %max.12, pred[128,1024]{0,1:T(8,128)(4,1)S(1)} %compare_and_fusion.2), kind=kLoop, calls=%fused_computation.10.clone.1 | loop fusion | flops 16773120 | bytes 16941056 | tf_op jit(solution)/shard_map/while/body/eval_jaxpr/reduce_sum | solution.py:79
  210.2 7.4 %fusion.72 = f32[8,4,128,64]{2,3,1,0:T(8,128)S(1)} fusion(bf16[1024,8,64,1]{0,2,3,1:T(8,128)(2,1)S(1)} %bitcast.98, f32[8,1024,128,4]{2,1,3,0:T(8,128)} %get-tuple-element.355, f32[8,4,128]{2,1,0:T(4,128)S(1)} %max.12, pred[128,1024]{0,1:T(8,128)(4,1)S(1)} %compare_and_fusion.2, f32[8,4,128,64]{2,3,1,0:T(8,128)S(1)} %get-tuple-element.376, ...), kind=kOutput, calls=%fused_computation.13.clone.1 | convolution fusion | flops 554434560 | bytes 20086784 | tf_op jit(solution)/shard_map/while/body/eval_jaxpr/kgqs,skd->kgqd/dot_general | solution.py:80
  226.9 9.1 %fusion.70 = f32[8,4,128]{2,1,0:T(4,128)S(1)} fusion(f32[8,1024,128,4]{2,1,3,0:T(8,128)} %get-tuple-element.355, f32[8,4,128]{2,1,0:T(4,128)S(1)} %max.12, pred[128,1024]{0,1:T(8,128)(4,1)S(1)} %compare_and_fusion.2), kind=kLoop, calls=%fused_computation.10.clone.1 | loop fusion | flops 16773120 | bytes 16941056 | tf_op jit(solution)/shard_map/while/body/eval_jaxpr/reduce_sum | solution.py:79
  236.1 7.4 %fusion.72 = f32[8,4,128,64]{2,3,1,0:T(8,128)S(1)} fusion(bf16[1024,8,64,1]{0,2,3,1:T(8,128)(2,1)S(1)} %bitcast.98, f32[8,1024,128,4]{2,1,3,0:T(8,128)} %get-tuple-element.355, f32[8,4,128]{2,1,0:T(4,128)S(1)} %max.12, pred[128,1024]{0,1:T(8,128)(4,1)S(1)} %compare_and_fusion.2, f32[8,4,128,64]{2,3,1,0:T(8,128)S(1)} %get-tuple-element.376, ...), kind=kOutput, calls=%fused_computation.13.clone.1 | convolution fusion | flops 554434560 | bytes 20086784 | tf_op jit(solution)/shard_map/while/body/eval_jaxpr/kgqs,skd->kgqd/dot_general | solution.py:80
  252.8 9.1 %fusion.70 = f32[8,4,128]{2,1,0:T(4,128)S(1)} fusion(f32[8,1024,128,4]{2,1,3,0:T(8,128)} %get-tuple-element.355, f32[8,4,128]{2,1,0:T(4,128)S(1)} %max.12, pred[128,1024]{0,1:T(8,128)(4,1)S(1)} %compare_and_fusion.2), kind=kLoop, calls=%fused_computation.10.clone.1 | loop fusion | flops 16773120 | bytes 16941056 | tf_op jit(solution)/shard_map/while/body/eval_jaxpr/reduce_sum | solution.py:79
  261.9 7.4 %fusion.72 = f32[8,4,128,64]{2,3,1,0:T(8,128)S(1)} fusion(bf16[1024,8,64,1]{0,2,3,1:T(8,128)(2,1)S(1)} %bitcast.98, f32[8,1024,128,4]{2,1,3,0:T(8,128)} %get-tuple-element.355, f32[8,4,128]{2,1,0:T(4,128)S(1)} %max.12, pred[128,1024]{0,1:T(8,128)(4,1)S(1)} %compare_and_fusion.2, f32[8,4,128,64]{2,3,1,0:T(8,128)S(1)} %get-tuple-element.376, ...), kind=kOutput, calls=%fused_computation.13.clone.1 | convolution fusion | flops 554434560 | bytes 20086784 | tf_op jit(solution)/shard_map/while/body/eval_jaxpr/kgqs,skd->kgqd/dot_general | solution.py:80
  269.7 7.7 %fusion.35 = (f32[128]{0:T(128)S(1)}, bf16[128,2880]{0,1:T(8,128)(2,1)S(1)}) fusion(bf16[2048,2880]{0,1:T(8,128)(2,1)} %all-gather.5.cloned.1.call-done, bf16[128,2048]{0,1:T(8,128)(2,1)S(1)} %bitcast.102, bf16[1,128,2880]{1,2,0:T(8,128)(2,1)} %param.14), kind=kOutput, calls=%fused_computation.55 | convolution fusion | flops 1512161152 | bytes 13795840 | tf_op jit(solution)/shard_map/dot_general | solution.py:109
  279.1 16.4 %scatter_custom_fusion = bf16[640,2880]{1,0:T(8,128)(2,1)} fusion(s32[512]{0:T(512)S(1)} %bitcast.106, bf16[128,2880]{1,0:T(8,128)(2,1)S(1)} %copy.54, s32[1024]{0:T(1024)S(1)} %pad_clamp_fusion.1, bf16[]{:T(256)} %constant.176.clone.1), kind=kCustom, calls=%fused_computation.47 | custom fusion | bytes 3686402 | tf_op jit(solution)/shard_map/scatter | solution.py:136
  295.6 7.3 broadcast_in_dim.138
  307.4 142.9 %all_to_all.10 = bf16[128,10,2880]{2,1,0:T(8,128)(2,1)} all-to-all(bf16[128,10,2880]{2,1,0:T(8,128)(2,1)S(1)} %bitcast.97), channel_id=1, replica_groups=mesh['ctx'=16,'grp'=8] {'ctx','grp'}, dimensions={0} | all-to-all | bytes 14745600 | tf_op jit(solution)/shard_map/all_to_all | solution.py:144
  450.2 14.4 %reshape.320 = bf16[1280,2880]{1,0:T(8,128)(2,1)} reshape(bf16[128,10,2880]{2,1,0:T(8,128)(2,1)} %all_to_all.10) | data formatting | bytes 14745600 | tf_op jit(solution)/shard_map/reshape | solution.py:145
  464.6 17.2 %fusion.22 = f32[1280,1536]{1,0:T(8,128)S(1)} fusion(bf16[1280,2880]{1,0:T(8,128)(2,1)} %reshape.320, bf16[1,2880,1536]{2,1,0:T(8,128)(2,1)} %param.24), kind=kOutput, calls=%fused_computation.37 | convolution fusion | flops 11324620800 | bytes 24084480 | tf_op jit(solution)/shard_map/dot_general | solution.py:146
  481.9 11.8 %convolution_convert_fusion = bf16[1280,2880]{0,1:T(8,128)(2,1)} fusion(bf16[1,768,2880]{1,2,0:T(8,128)(2,1)} %param.25, f32[1280,1536]{1,0:T(8,128)S(1)} %fusion.22), kind=kOutput, calls=%fused_computation.36 | convolution fusion | flops 5673861120 | bytes 19660800 | tf_op jit(solution)/shard_map/dot_general | solution.py:148
  493.6 10.4 %copy.55 = bf16[1280,2880]{1,0:T(8,128)(2,1)} copy(bf16[1280,2880]{0,1:T(8,128)(2,1)} %convolution_convert_fusion) | data formatting | bytes 14745600 | tf_op jit(solution)/shard_map/convert_element_type | solution.py:148
  504.1 13.4 %reshape.321 = bf16[128,10,2880]{2,1,0:T(8,128)(2,1)} reshape(bf16[1280,2880]{1,0:T(8,128)(2,1)} %copy.55) | data formatting | bytes 14745600 | tf_op jit(solution)/shard_map/reshape | solution.py:151
  517.5 12.0 %all-to-all-start.1 = ((bf16[128,10,2880]{2,1,0:T(8,128)(2,1)}), bf16[128,10,2880]{2,1,0:T(8,128)(2,1)}, u32[]{:S(2)}, u32[]{:S(2)}) async-start(bf16[128,10,2880]{2,1,0:T(8,128)(2,1)} %reshape.321), calls=%async_computation.1 | async-start | bytes 24117248 | tf_op jit(solution)/shard_map/all_to_all | solution.py:152
  530.0 157.7 %all-to-all-done.1 = bf16[128,10,2880]{2,1,0:T(8,128)(2,1)} async-done(((bf16[128,10,2880]{2,1,0:T(8,128)(2,1)}), bf16[128,10,2880]{2,1,0:T(8,128)(2,1)}, u32[]{:S(2)}, u32[]{:S(2)}) %all-to-all-start.1) | async-done | bytes 7372832 | tf_op jit(solution)/shard_map/all_to_all | solution.py:152
  687.7 14.7 %bitcast_reduce_fusion = bf16[64,10,2880]{2,1,0:T(8,128)(2,1)} fusion(bf16[128,10,2880]{2,1,0:T(8,128)(2,1)} %all-to-all-done.1), kind=kLoop, calls=%fused_computation.35 | loop fusion | flops 1843200 | bytes 11059200 | tf_op jit(solution)/shard_map/reduce_sum | solution.py:153
  702.4 7.8 %reshape.323 = bf16[640,2880]{1,0:T(8,128)(2,1)} reshape(bf16[64,10,2880]{2,1,0:T(8,128)(2,1)} %bitcast_reduce_fusion) | data formatting | bytes 7372800 | tf_op jit(solution)/shard_map/reshape | solution.py:154
  710.2 8.4 %gather_fusion = bf16[512,2880]{1,0:T(8,128)(2,1)S(1)} fusion(bf16[640,2880]{1,0:T(8,128)(2,1)} %reshape.323, s32[1024]{0:T(1024)S(1)} %pad_clamp_fusion), kind=kCustom, calls=%fused_computation.1 | custom fusion | bytes 5900288 | tf_op jit(solution)/shard_map/gather | solution.py:155
  (114 shorter events, 54.9 us)
Async XLA Ops:
  7.2 522.4 %copy-start = (bf16[2880,64]{0,1:T(8,128)(2,1)S(1)}, bf16[2880,64]{0,1:T(8,128)(2,1)}, u32[]{:S(2)}) copy-start(bf16[2880,64]{0,1:T(8,128)(2,1)} %param.22) | copy-start | bytes 1105924
  7.2 4.3 copy-start.3
  7.2 4.7 copy-start.6
  7.2 4.8 copy-start.7
  7.2 5.1 copy-start.2
  7.2 104.5 %all-gather.3.cloned.1.call-start = ((), (), s32[]{:S(2)}) async-start(), calls=%async_computation.2 | async-start | bytes 13369344 | tf_op jit(solution)/shard_map/all_gather | solution.py:91
  10.7 259.0 %all-gather.5.cloned.1.call-start = ((), (), s32[]{:S(2)}) async-start(), calls=%async_computation.3 | async-start | bytes 12533760 | tf_op jit(solution)/shard_map/all_gather | solution.py:111
  269.7 8.6 %copy-start.5 = (f32[2880]{0:T(1024)S(1)}, f32[2880]{0:T(1024)}, u32[]{:S(2)}) copy-start(f32[2880]{0:T(1024)} %param.21) | copy-start | bytes 34564
  277.5 0.9 copy-start.1
  517.5 12.3 %copy-start.4 = (s32[1,128,4]{1,2,0:T(4,128)S(1)}, s32[1,128,4]{1,2,0:T(4,128)}, u32[]{:S(2)}) copy-start(s32[1,128,4]{1,2,0:T(4,128)} %param.23) | copy-start | bytes 6148
  517.5 170.2 %all-to-all-start.1 = ((bf16[128,10,2880]{2,1,0:T(8,128)(2,1)}), bf16[128,10,2880]{2,1,0:T(8,128)(2,1)}, u32[]{:S(2)}, u32[]{:S(2)}) async-start(bf16[128,10,2880]{2,1,0:T(8,128)(2,1)} %reshape.321), calls=%async_computation.1 | async-start | bytes 24117248 | tf_op jit(solution)/shard_map/all_to_all | solution.py:152
Sparse Core Ops, SparseCore 0:
  10.8 100.8 all-gather.2
  113.8 94.9 all-gather.4
where the time goes:
time: 747 us; the launch traced here: 739 us
  waiting for transfers between devices  256 us (34%)
  blocking collectives  143 us (19%)
  matrix products  125 us (17%)
  local copies, waits for them, and re-layouts  102 us (14%)
  other arithmetic  86.3 us (12%)
  between operations  14.6 us (2%)
  starting transfers between devices  12.1 us (2%)
    all_to_all x1, waiting for transfers between devices, body(): lax.all_to_all(partial_out, ('ctx', 'grp'), split_axis=0, concat_axis=0,...  158 us
    all_to_all x1, blocking collectives, body(): lax.all_to_all(doubled, ('ctx', 'grp'), split_axis=0, concat_axis=0, tile...  143 us
    all_gather x1, waiting for transfers between devices, body(): piece = lax.all_gather(local_kv, 'ctx', axis=0, tiled=True)  97.2 us
    reduce_sum x6, other arithmetic, key_block(): total = total * shrink + jnp.sum(weights, axis=-1)  56 us
    dot_general x6, matrix products, key_block(): jnp.einsum('kgqs,skd->kgqd', weights.astype(jnp.bfloat16), values, prefer...  45 us
    dot_general x6, matrix products, key_block(): jnp.einsum('qkgd,skd->kgqs', query_heads, keys, preferred_element_type=jn...  42.7 us
    dot_general x1, matrix products, body(): pre = jnp.dot(flat_rows, in_weights, preferred_element_type=jnp.float32)  17.2 us
    scatter x1, local copies, waits for them, and re-layouts, body(): jnp.zeros((experts * capacity, width), jnp.bfloat16).at[dest]  16.4 us
  transfers between devices with their start and end apart: 3, of which 2 were waited for; matrix products, arithmetic and copies ran while one was open for 22% of the time, Pallas kernels for 0%

commit v1 on v0

--- a/solution.py
+++ b/solution.py
@@ -88,7 +88,16 @@
     start_top = jnp.broadcast_to(sink_grid[:, :, None], (KVH, groups, tokens))
     start_total = jnp.zeros((KVH, groups, tokens), jnp.float32)
     start_numer = jnp.zeros((KVH, groups, tokens, HD), jnp.float32)
-    piece = lax.all_gather(local_kv, "ctx", axis=0, tiled=True)
+    ways = lax.axis_size("ctx")
+    up = [(d, (d + 1) % ways) for d in range(ways)]
+    down = [(d, (d - 1) % ways) for d in range(ways)]
+    earlier, later = ([local_kv], [local_kv])
+    for _ in range(ways // 2):
+        earlier.append(lax.ppermute(earlier[-1], "ctx", up))
+    for _ in range((ways - 1) // 2):
+        later.append(lax.ppermute(later[-1], "ctx", down))
+    line = jnp.concatenate([*earlier[::-1], *later[1:]], axis=0)
+    piece = jnp.roll(line, (lax.axis_index("ctx") - ways // 2) * local_kv.shape[0], axis=0)
     count = piece.shape[0]
     step_rows = math.gcd(count, 1024)
 

time: 747 us -> 844 us (1.13)
  starting transfers between devices: 12.1 us -> 55.4 us
  local copies, waits for them, and re-layouts: 102 us -> 137 us
  waiting for transfers between devices: 256 us -> 272 us
    ppermute x0 -> x15, waiting for transfers between devices: none -> 114 us  [the longest x8 102 us: body(): earlier.append(lax.ppermute(earlier[-1], 'ctx', up))]
    all_gather x1 -> x0, waiting for transfers between devices: 97.2 us -> none  [body(): piece = lax.all_gather(local_kv, 'ctx', axis=0, tiled=True)]
    ppermute x0 -> x15, starting transfers between devices: none -> 43.3 us  [the longest x7 40.2 us: body(): later.append(lax.ppermute(later[-1], 'ctx', down))]
    unnamed x20 -> x71, local copies, waits for them, and re-layouts: 3.72 us -> 26.9 us
    dynamic_slice x0 -> x1, local copies, waits for them, and re-layouts: none -> 11 us  [body(): jnp.roll(line, (lax.axis_index('ctx') - ways // 2) * local_kv.shape[0], a...]
  transfers between devices with their start and end apart: 3 -> 17, of which waited for: 2 -> 10; matrix products, arithmetic and copies ran while one was open for 22% -> 24% of each run, Pallas kernels for 0% -> 0%
where the time goes in v1:
time: 844 us; the launch traced here: 835 us
  waiting for transfers between devices  272 us (32%)
  blocking collectives  144 us (17%)
  local copies, waits for them, and re-layouts  137 us (16%)
  matrix products  124 us (15%)
  other arithmetic  86.6 us (10%)
  starting transfers between devices  55.4 us (7%)
  between operations  15.3 us (2%)
    all_to_all x1, waiting for transfers between devices, body(): lax.all_to_all(partial_out, ('ctx', 'grp'), split_axis=0, concat_axis=0,...  158 us
    all_to_all x1, blocking collectives, body(): lax.all_to_all(doubled, ('ctx', 'grp'), split_axis=0, concat_axis=0, tile...  144 us
    ppermute x8, waiting for transfers between devices, body(): earlier.append(lax.ppermute(earlier[-1], 'ctx', up))  102 us
    reduce_sum x6, other arithmetic, key_block(): total = total * shrink + jnp.sum(weights, axis=-1)  55.2 us
    dot_general x6, matrix products, key_block(): jnp.einsum('kgqs,skd->kgqd', weights.astype(jnp.bfloat16), values, prefer...  44.4 us
    dot_general x6, matrix products, key_block(): jnp.einsum('qkgd,skd->kgqs', query_heads, keys, preferred_element_type=jn...  42.7 us
    ppermute x7, starting transfers between devices, body(): later.append(lax.ppermute(later[-1], 'ctx', down))  40.2 us
    unnamed x71, local copies, waits for them, and re-layouts  26.9 us
  transfers between devices with their start and end apart: 17, of which 10 were waited for; matrix products, arithmetic and copies ran while one was open for 24% of the time, Pallas kernels for 0%

profile of v1, /device:TPU:66, one launch (start us, length us, event | category | flops | bytes accessed | tf_op | source)
XLA Modules:
  0.0 835.3 jit_solution(15397931724016249860)
XLA Ops:
  11.3 17.8 %collective-permute-done = bf16[384,1024]{0,1:T(8,128)(2,1)S(1)} collective-permute-done((bf16[384,1024]{0,1:T(8,128)(2,1)S(1)}, bf16[384,1024]{0,1:T(8,128)(2,1)S(1)}, u32[]{:S(2)}, u32[]{:S(2)}) %collective-permute-start) | collective-permute-done | bytes 786464 | tf_op jit(solution)/shard_map/ppermute | solution.py:96
  33.1 16.8 %collective-permute-done.1 = bf16[384,1024]{0,1:T(8,128)(2,1)S(1)} collective-permute-done((bf16[384,1024]{0,1:T(8,128)(2,1)S(1)}, bf16[384,1024]{0,1:T(8,128)(2,1)S(1)}, u32[]{:S(2)}, u32[]{:S(2)}) %collective-permute-start.1) | collective-permute-done | bytes 786464 | tf_op jit(solution)/shard_map/ppermute | solution.py:96
  55.1 15.8 %collective-permute-done.2 = bf16[384,1024]{0,1:T(8,128)(2,1)S(1)} collective-permute-done((bf16[384,1024]{0,1:T(8,128)(2,1)S(1)}, bf16[384,1024]{0,1:T(8,128)(2,1)S(1)}, u32[]{:S(2)}, u32[]{:S(2)}) %collective-permute-start.2) | collective-permute-done | bytes 786464 | tf_op jit(solution)/shard_map/ppermute | solution.py:96
  76.1 14.9 %collective-permute-done.3 = bf16[384,1024]{0,1:T(8,128)(2,1)S(1)} collective-permute-done((bf16[384,1024]{0,1:T(8,128)(2,1)S(1)}, bf16[384,1024]{0,1:T(8,128)(2,1)S(1)}, u32[]{:S(2)}, u32[]{:S(2)}) %collective-permute-start.3) | collective-permute-done | bytes 786464 | tf_op jit(solution)/shard_map/ppermute | solution.py:96
  96.1 14.0 %collective-permute-done.4 = bf16[384,1024]{0,1:T(8,128)(2,1)S(1)} collective-permute-done((bf16[384,1024]{0,1:T(8,128)(2,1)S(1)}, bf16[384,1024]{0,1:T(8,128)(2,1)S(1)}, u32[]{:S(2)}, u32[]{:S(2)}) %collective-permute-start.4) | collective-permute-done | bytes 786464 | tf_op jit(solution)/shard_map/ppermute | solution.py:96
  115.3 13.2 %collective-permute-done.5 = bf16[384,1024]{0,1:T(8,128)(2,1)} collective-permute-done((bf16[384,1024]{0,1:T(8,128)(2,1)S(1)}, bf16[384,1024]{0,1:T(8,128)(2,1)}, u32[]{:S(2)}, u32[]{:S(2)}) %collective-permute-start.5) | collective-permute-done | bytes 786464 | tf_op jit(solution)/shard_map/ppermute | solution.py:96
  146.4 12.4 %collective-permute-done.13 = bf16[384,1024]{0,1:T(8,128)(2,1)S(1)} collective-permute-done((bf16[384,1024]{0,1:T(8,128)(2,1)}, bf16[384,1024]{0,1:T(8,128)(2,1)S(1)}, u32[]{:S(2)}, u32[]{:S(2)}) %collective-permute-start.13) | collective-permute-done | bytes 786464 | tf_op jit(solution)/shard_map/ppermute | solution.py:98
  158.7 12.0 %collective-permute-start.14 = (bf16[384,1024]{0,1:T(8,128)(2,1)S(1)}, bf16[384,1024]{0,1:T(8,128)(2,1)S(1)}, u32[]{:S(2)}, u32[]{:S(2)}) collective-permute-start(bf16[384,1024]{0,1:T(8,128)(2,1)S(1)} %collective-permute-done.13), channel_id=1, source_target_pairs={{0,120},{8,0},{16,8},{24,16},{32,24},{40,32},{48,40},{56,48},{64,5... | collective-permute-start | bytes 2359304 | tf_op jit(solution)/shard_map/ppermute | solution.py:98
  196.7 11.0 %constant_dynamic-slice_fusion.1 = bf16[6144,1024]{0,1:T(8,128)(2,1)} fusion(bf16[12288,1024]{0,1:T(8,128)(2,1)S(1)} %constant_dynamic-update-slice_fusion, s32[]{:T(128)S(6)} %select_n.162), kind=kLoop, calls=%fused_computation.121 | loop fusion | bytes 25165828 | tf_op jit(solution)/shard_map/jit(_roll_dynamic)/dynamic_slice | solution.py:100
  207.8 156.5 %while.20 = (s32[]{:T(128)}, f32[8,4,128]{2,1,0:T(4,128)S(1)}, f32[8,4,128]{2,1,0:T(4,128)S(1)}, f32[8,4,128,64]{2,3,1,0:T(8,128)S(1)}, s32[1,8]{1,0:T(1,128)S(1...) while((s32[]{:T(128)}, f32[8,4,128]{2,1,0:T(4,128)S(1)}, ...), condition=%wide.region_7.8_spmd.clone, body=%wide.region_3.7_spmd.clone.sunk | while | flops 1121116288 | bytes 60053240 | solution.py:109
  217.2 9.8 %fusion.70 = f32[8,4,128]{2,1,0:T(4,128)S(1)} fusion(f32[8,1024,128,4]{2,1,3,0:T(8,128)} %get-tuple-element.355, f32[8,4,128]{2,1,0:T(4,128)S(1)} %max.12, pred[128,1024]{0,1:T(8,128)(4,1)S(1)} %compare_and_fusion.2), kind=kLoop, calls=%fused_computation.10.clone.1 | loop fusion | flops 16773120 | bytes 16941056 | tf_op jit(solution)/shard_map/while/body/eval_jaxpr/reduce_sum | solution.py:79
  244.0 9.1 %fusion.70 = f32[8,4,128]{2,1,0:T(4,128)S(1)} fusion(f32[8,1024,128,4]{2,1,3,0:T(8,128)} %get-tuple-element.355, f32[8,4,128]{2,1,0:T(4,128)S(1)} %max.12, pred[128,1024]{0,1:T(8,128)(4,1)S(1)} %compare_and_fusion.2), kind=kLoop, calls=%fused_computation.10.clone.1 | loop fusion | flops 16773120 | bytes 16941056 | tf_op jit(solution)/shard_map/while/body/eval_jaxpr/reduce_sum | solution.py:79
  253.2 7.4 fusion.72
  269.8 9.1 %fusion.70 = f32[8,4,128]{2,1,0:T(4,128)S(1)} fusion(f32[8,1024,128,4]{2,1,3,0:T(8,128)} %get-tuple-element.355, f32[8,4,128]{2,1,0:T(4,128)S(1)} %max.12, pred[128,1024]{0,1:T(8,128)(4,1)S(1)} %compare_and_fusion.2), kind=kLoop, calls=%fused_computation.10.clone.1 | loop fusion | flops 16773120 | bytes 16941056 | tf_op jit(solution)/shard_map/while/body/eval_jaxpr/reduce_sum | solution.py:79
  279.0 7.4 fusion.72
  295.7 9.1 %fusion.70 = f32[8,4,128]{2,1,0:T(4,128)S(1)} fusion(f32[8,1024,128,4]{2,1,3,0:T(8,128)} %get-tuple-element.355, f32[8,4,128]{2,1,0:T(4,128)S(1)} %max.12, pred[128,1024]{0,1:T(8,128)(4,1)S(1)} %compare_and_fusion.2), kind=kLoop, calls=%fused_computation.10.clone.1 | loop fusion | flops 16773120 | bytes 16941056 | tf_op jit(solution)/shard_map/while/body/eval_jaxpr/reduce_sum | solution.py:79
  321.5 9.1 %fusion.70 = f32[8,4,128]{2,1,0:T(4,128)S(1)} fusion(f32[8,1024,128,4]{2,1,3,0:T(8,128)} %get-tuple-element.355, f32[8,4,128]{2,1,0:T(4,128)S(1)} %max.12, pred[128,1024]{0,1:T(8,128)(4,1)S(1)} %compare_and_fusion.2), kind=kLoop, calls=%fused_computation.10.clone.1 | loop fusion | flops 16773120 | bytes 16941056 | tf_op jit(solution)/shard_map/while/body/eval_jaxpr/reduce_sum | solution.py:79
  330.6 7.4 fusion.72
  347.3 9.1 %fusion.70 = f32[8,4,128]{2,1,0:T(4,128)S(1)} fusion(f32[8,1024,128,4]{2,1,3,0:T(8,128)} %get-tuple-element.355, f32[8,4,128]{2,1,0:T(4,128)S(1)} %max.12, pred[128,1024]{0,1:T(8,128)(4,1)S(1)} %compare_and_fusion.2), kind=kLoop, calls=%fused_computation.10.clone.1 | loop fusion | flops 16773120 | bytes 16941056 | tf_op jit(solution)/shard_map/while/body/eval_jaxpr/reduce_sum | solution.py:79
  364.6 7.7 fusion.35
  374.0 16.4 %scatter_custom_fusion = bf16[640,2880]{1,0:T(8,128)(2,1)} fusion(s32[512]{0:T(512)S(1)} %bitcast.110, bf16[128,2880]{1,0:T(8,128)(2,1)S(1)} %copy.54, s32[1024]{0:T(1024)S(1)} %pad_clamp_fusion.1, bf16[]{:T(256)} %constant.199.clone.1), kind=kCustom, calls=%fused_computation.47 | custom fusion | bytes 3686402 | tf_op jit(solution)/shard_map/scatter | solution.py:145
  402.2 144.0 %all_to_all.10 = bf16[128,10,2880]{2,1,0:T(8,128)(2,1)} all-to-all(bf16[128,10,2880]{2,1,0:T(8,128)(2,1)S(1)} %bitcast.101), channel_id=1, replica_groups=mesh['ctx'=16,'grp'=8] {'ctx','grp'}, dimensions={0} | all-to-all | bytes 14745600 | tf_op jit(solution)/shard_map/all_to_all | solution.py:153
  546.2 14.4 %reshape.320 = bf16[1280,2880]{1,0:T(8,128)(2,1)} reshape(bf16[128,10,2880]{2,1,0:T(8,128)(2,1)} %all_to_all.10) | data formatting | bytes 14745600 | tf_op jit(solution)/shard_map/reshape | solution.py:154
  560.5 17.2 %fusion.22 = f32[1280,1536]{1,0:T(8,128)S(1)} fusion(bf16[1280,2880]{1,0:T(8,128)(2,1)} %reshape.320, bf16[1,2880,1536]{2,1,0:T(8,128)(2,1)} %param.24), kind=kOutput, calls=%fused_computation.37 | convolution fusion | flops 11324620800 | bytes 24084480 | tf_op jit(solution)/shard_map/dot_general | solution.py:155
  577.8 11.8 %convolution_convert_fusion = bf16[1280,2880]{0,1:T(8,128)(2,1)} fusion(bf16[1,768,2880]{1,2,0:T(8,128)(2,1)} %param.25, f32[1280,1536]{1,0:T(8,128)S(1)} %fusion.22), kind=kOutput, calls=%fused_computation.36 | convolution fusion | flops 5673861120 | bytes 19660800 | tf_op jit(solution)/shard_map/dot_general | solution.py:157
  589.6 10.4 %copy.55 = bf16[1280,2880]{1,0:T(8,128)(2,1)} copy(bf16[1280,2880]{0,1:T(8,128)(2,1)} %convolution_convert_fusion) | data formatting | bytes 14745600 | tf_op jit(solution)/shard_map/convert_element_type | solution.py:157
  600.0 13.4 %reshape.321 = bf16[128,10,2880]{2,1,0:T(8,128)(2,1)} reshape(bf16[1280,2880]{1,0:T(8,128)(2,1)} %copy.55) | data formatting | bytes 14745600 | tf_op jit(solution)/shard_map/reshape | solution.py:160
  613.4 12.1 %all-to-all-start.1 = ((bf16[128,10,2880]{2,1,0:T(8,128)(2,1)}), bf16[128,10,2880]{2,1,0:T(8,128)(2,1)}, u32[]{:S(2)}, u32[]{:S(2)}) async-start(bf16[128,10,2880]{2,1,0:T(8,128)(2,1)} %reshape.321), calls=%async_computation.1 | async-start | bytes 24117248 | tf_op jit(solution)/shard_map/all_to_all | solution.py:161
  626.0 157.7 %all-to-all-done.1 = bf16[128,10,2880]{2,1,0:T(8,128)(2,1)} async-done(((bf16[128,10,2880]{2,1,0:T(8,128)(2,1)}), bf16[128,10,2880]{2,1,0:T(8,128)(2,1)}, u32[]{:S(2)}, u32[]{:S(2)}) %all-to-all-start.1) | async-done | bytes 7372832 | tf_op jit(solution)/shard_map/all_to_all | solution.py:161
  783.7 14.7 %bitcast_reduce_fusion = bf16[64,10,2880]{2,1,0:T(8,128)(2,1)} fusion(bf16[128,10,2880]{2,1,0:T(8,128)(2,1)} %all-to-all-done.1), kind=kLoop, calls=%fused_computation.35 | loop fusion | flops 1843200 | bytes 11059200 | tf_op jit(solution)/shard_map/reduce_sum | solution.py:162
  798.4 7.8 reshape.323
  806.2 8.4 %gather_fusion = bf16[512,2880]{1,0:T(8,128)(2,1)S(1)} fusion(bf16[640,2880]{1,0:T(8,128)(2,1)} %reshape.323, s32[1024]{0:T(1024)S(1)} %pad_clamp_fusion), kind=kCustom, calls=%fused_computation.1 | custom fusion | bytes 5900288 | tf_op jit(solution)/shard_map/gather | solution.py:164
  (194 shorter events, 177.9 us)
Async XLA Ops:
  7.2 618.4 %copy-start = (bf16[2880,64]{0,1:T(8,128)(2,1)S(1)}, bf16[2880,64]{0,1:T(8,128)(2,1)}, u32[]{:S(2)}) copy-start(bf16[2880,64]{0,1:T(8,128)(2,1)} %param.22) | copy-start | bytes 1105924
  7.2 357.4 %all-gather.2.cloned.1.call-start = ((), (), s32[]{:S(2)}) async-start(), calls=%async_computation.2 | async-start | bytes 12533760 | tf_op jit(solution)/shard_map/all_gather | solution.py:120
  9.7 19.4 %collective-permute-start = (bf16[384,1024]{0,1:T(8,128)(2,1)S(1)}, bf16[384,1024]{0,1:T(8,128)(2,1)S(1)}, u32[]{:S(2)}, u32[]{:S(2)}) collective-permute-start(bf16[384,1024]{0,1:T(8,128)(2,1)S(1)} %pad_maximum_fusion), channel_id=1, source_target_pairs={{0,8},{8,16},{16,24},{24,32},{32,40},{40,48},{48,56},{56,64},{64,7... | collective-permute-start | bytes 2359304 | tf_op jit(solution)/shard_map/ppermute | solution.py:96
  29.1 20.8 %collective-permute-start.1 = (bf16[384,1024]{0,1:T(8,128)(2,1)S(1)}, bf16[384,1024]{0,1:T(8,128)(2,1)S(1)}, u32[]{:S(2)}, u32[]{:S(2)}) collective-permute-start(bf16[384,1024]{0,1:T(8,128)(2,1)S(1)} %collective-permute-done), channel_id=1, source_target_pairs={{0,8},{8,16},{16,24},{24,32},{32,40},{40,48},{48,56},{56,64},{64,7... | collective-permute-start | bytes 2359304 | tf_op jit(solution)/shard_map/ppermute | solution.py:96
  30.6 19.4 %collective-permute-start.8 = (bf16[384,1024]{0,1:T(8,128)(2,1)S(1)}, bf16[384,1024]{0,1:T(8,128)(2,1)S(1)}, u32[]{:S(2)}, u32[]{:S(2)}) collective-permute-start(bf16[384,1024]{0,1:T(8,128)(2,1)S(1)} %pad_maximum_fusion), channel_id=1, source_target_pairs={{0,120},{8,0},{16,8},{24,16},{32,24},{40,32},{48,40},{56,48},{64,5... | collective-permute-start | bytes 2359304 | tf_op jit(solution)/shard_map/ppermute | solution.py:98
  49.9 21.0 %copy-start.1 = (bf16[384,1024]{0,1:T(8,128)(2,1)}, bf16[384,1024]{0,1:T(8,128)(2,1)S(1)}, u32[]{:S(2)}) copy-start(bf16[384,1024]{0,1:T(8,128)(2,1)S(1)} %collective-permute-done.1) | copy-start | bytes 2359300
  49.9 21.0 %collective-permute-start.2 = (bf16[384,1024]{0,1:T(8,128)(2,1)S(1)}, bf16[384,1024]{0,1:T(8,128)(2,1)S(1)}, u32[]{:S(2)}, u32[]{:S(2)}) collective-permute-start(bf16[384,1024]{0,1:T(8,128)(2,1)S(1)} %collective-permute-done.1), channel_id=1, source_target_pairs={{0,8},{8,16},{16,24},{24,32},{32,40},{40,48},{48,56},{56,64},{64,7... | collective-permute-start | bytes 2359304 | tf_op jit(solution)/shard_map/ppermute | solution.py:96
  49.9 21.0 %collective-permute-start.9 = (bf16[384,1024]{0,1:T(8,128)(2,1)S(1)}, bf16[384,1024]{0,1:T(8,128)(2,1)S(1)}, u32[]{:S(2)}, u32[]{:S(2)}) collective-permute-start(bf16[384,1024]{0,1:T(8,128)(2,1)S(1)} %collective-permute-done.8), channel_id=1, source_target_pairs={{0,120},{8,0},{16,8},{24,16},{32,24},{40,32},{48,40},{56,48},{64,5... | collective-permute-start | bytes 2359304 | tf_op jit(solution)/shard_map/ppermute | solution.py:98
  70.9 20.1 %copy-start.5 = (bf16[384,1024]{0,1:T(8,128)(2,1)}, bf16[384,1024]{0,1:T(8,128)(2,1)S(1)}, u32[]{:S(2)}) copy-start(bf16[384,1024]{0,1:T(8,128)(2,1)S(1)} %collective-permute-done.2) | copy-start | bytes 2359300
  70.9 20.1 %collective-permute-start.3 = (bf16[384,1024]{0,1:T(8,128)(2,1)S(1)}, bf16[384,1024]{0,1:T(8,128)(2,1)S(1)}, u32[]{:S(2)}, u32[]{:S(2)}) collective-permute-start(bf16[384,1024]{0,1:T(8,128)(2,1)S(1)} %collective-permute-done.2), channel_id=1, source_target_pairs={{0,8},{8,16},{16,24},{24,32},{32,40},{40,48},{48,56},{56,64},{64,7... | collective-permute-start | bytes 2359304 | tf_op jit(solution)/shard_map/ppermute | solution.py:96
  70.9 5.1 copy-start.3
  70.9 20.0 %collective-permute-start.10 = (bf16[384,1024]{0,1:T(8,128)(2,1)S(1)}, bf16[384,1024]{0,1:T(8,128)(2,1)S(1)}, u32[]{:S(2)}, u32[]{:S(2)}) collective-permute-start(bf16[384,1024]{0,1:T(8,128)(2,1)S(1)} %collective-permute-done.9), channel_id=1, source_target_pairs={{0,120},{8,0},{16,8},{24,16},{32,24},{40,32},{48,40},{56,48},{64,5... | collective-permute-start | bytes 2359304 | tf_op jit(solution)/shard_map/ppermute | solution.py:98
  91.0 19.2 %copy-start.9 = (bf16[384,1024]{0,1:T(8,128)(2,1)}, bf16[384,1024]{0,1:T(8,128)(2,1)S(1)}, u32[]{:S(2)}) copy-start(bf16[384,1024]{0,1:T(8,128)(2,1)S(1)} %collective-permute-done.3) | copy-start | bytes 2359300
  91.0 19.1 %collective-permute-start.4 = (bf16[384,1024]{0,1:T(8,128)(2,1)S(1)}, bf16[384,1024]{0,1:T(8,128)(2,1)S(1)}, u32[]{:S(2)}, u32[]{:S(2)}) collective-permute-start(bf16[384,1024]{0,1:T(8,128)(2,1)S(1)} %collective-permute-done.3), channel_id=1, source_target_pairs={{0,8},{8,16},{16,24},{24,32},{32,40},{40,48},{48,56},{56,64},{64,7... | collective-permute-start | bytes 2359304 | tf_op jit(solution)/shard_map/ppermute | solution.py:96
  91.0 19.1 %collective-permute-start.11 = (bf16[384,1024]{0,1:T(8,128)(2,1)S(1)}, bf16[384,1024]{0,1:T(8,128)(2,1)}, u32[]{:S(2)}, u32[]{:S(2)}) collective-permute-start(bf16[384,1024]{0,1:T(8,128)(2,1)S(1)} %collective-permute-done.10), channel_id=1, source_target_pairs={{0,120},{8,0},{16,8},{24,16},{32,24},{40,32},{48,40},{56,48},{64,5... | collective-permute-start | bytes 2359304 | tf_op jit(solution)/shard_map/ppermute | solution.py:98
  110.1 5.2 copy-start.11
  110.1 18.3 %collective-permute-start.5 = (bf16[384,1024]{0,1:T(8,128)(2,1)S(1)}, bf16[384,1024]{0,1:T(8,128)(2,1)}, u32[]{:S(2)}, u32[]{:S(2)}) collective-permute-start(bf16[384,1024]{0,1:T(8,128)(2,1)S(1)} %collective-permute-done.4), channel_id=1, source_target_pairs={{0,8},{8,16},{16,24},{24,32},{32,40},{40,48},{48,56},{56,64},{64,7... | collective-permute-start | bytes 2359304 | tf_op jit(solution)/shard_map/ppermute | solution.py:96
  110.1 25.6 %collective-permute-start.12 = (bf16[384,1024]{0,1:T(8,128)(2,1)}, bf16[384,1024]{0,1:T(8,128)(2,1)}, u32[]{:S(2)}, u32[]{:S(2)}) collective-permute-start(bf16[384,1024]{0,1:T(8,128)(2,1)} %collective-permute-done.11), channel_id=1, source_target_pairs={{0,120},{8,0},{16,8},{24,16},{32,24},{40,32},{48,40},{56,48},{64,5... | collective-permute-start | bytes 2359304 | tf_op jit(solution)/shard_map/ppermute | solution.py:98
  128.4 17.7 %collective-permute-start.6 = (bf16[384,1024]{0,1:T(8,128)(2,1)}, bf16[384,1024]{0,1:T(8,128)(2,1)}, u32[]{:S(2)}, u32[]{:S(2)}) collective-permute-start(bf16[384,1024]{0,1:T(8,128)(2,1)} %collective-permute-done.5), channel_id=1, source_target_pairs={{0,8},{8,16},{16,24},{24,32},{32,40},{40,48},{48,56},{56,64},{64,7... | collective-permute-start | bytes 2359304 | tf_op jit(solution)/shard_map/ppermute | solution.py:96
  135.6 49.4 %copy-start.8 = (bf16[384,1024]{0,1:T(8,128)(2,1)S(1)}, bf16[384,1024]{0,1:T(8,128)(2,1)}, u32[]{:S(2)}) copy-start(bf16[384,1024]{0,1:T(8,128)(2,1)} %copy-done.7) | copy-start | bytes 2359300
  135.7 55.8 %copy-start.12 = (bf16[384,1024]{0,1:T(8,128)(2,1)S(1)}, bf16[384,1024]{0,1:T(8,128)(2,1)}, u32[]{:S(2)}) copy-start(bf16[384,1024]{0,1:T(8,128)(2,1)} %copy-done.11) | copy-start | bytes 2359300
  135.7 56.0 %copy-start.10 = (bf16[384,1024]{0,1:T(8,128)(2,1)S(1)}, bf16[384,1024]{0,1:T(8,128)(2,1)}, u32[]{:S(2)}) copy-start(bf16[384,1024]{0,1:T(8,128)(2,1)} %copy-done.9) | copy-start | bytes 2359300
  135.7 56.2 %copy-start.6 = (bf16[384,1024]{0,1:T(8,128)(2,1)S(1)}, bf16[384,1024]{0,1:T(8,128)(2,1)}, u32[]{:S(2)}) copy-start(bf16[384,1024]{0,1:T(8,128)(2,1)} %copy-done.5) | copy-start | bytes 2359300
  135.7 23.1 %collective-permute-start.13 = (bf16[384,1024]{0,1:T(8,128)(2,1)}, bf16[384,1024]{0,1:T(8,128)(2,1)S(1)}, u32[]{:S(2)}, u32[]{:S(2)}) collective-permute-start(bf16[384,1024]{0,1:T(8,128)(2,1)} %collective-permute-done.12), channel_id=1, source_target_pairs={{0,120},{8,0},{16,8},{24,16},{32,24},{40,32},{48,40},{56,48},{64,5... | collective-permute-start | bytes 2359304 | tf_op jit(solution)/shard_map/ppermute | solution.py:98
  146.1 28.5 %collective-permute-start.7 = (bf16[384,1024]{0,1:T(8,128)(2,1)}, bf16[384,1024]{0,1:T(8,128)(2,1)S(1)}, u32[]{:S(2)}, u32[]{:S(2)}) collective-permute-start(bf16[384,1024]{0,1:T(8,128)(2,1)} %collective-permute-done.6), channel_id=1, source_target_pairs={{0,8},{8,16},{16,24},{24,32},{32,40},{40,48},{48,56},{56,64},{64,7... | collective-permute-start | bytes 2359304 | tf_op jit(solution)/shard_map/ppermute | solution.py:96
  158.7 29.5 %collective-permute-start.14 = (bf16[384,1024]{0,1:T(8,128)(2,1)S(1)}, bf16[384,1024]{0,1:T(8,128)(2,1)S(1)}, u32[]{:S(2)}, u32[]{:S(2)}) collective-permute-start(bf16[384,1024]{0,1:T(8,128)(2,1)S(1)} %collective-permute-done.13), channel_id=1, source_target_pairs={{0,120},{8,0},{16,8},{24,16},{32,24},{40,32},{48,40},{56,48},{64,5... | collective-permute-start | bytes 2359304 | tf_op jit(solution)/shard_map/ppermute | solution.py:98
  174.8 17.4 %copy-start.2 = (bf16[384,1024]{0,1:T(8,128)(2,1)S(1)}, bf16[384,1024]{0,1:T(8,128)(2,1)}, u32[]{:S(2)}) copy-start(bf16[384,1024]{0,1:T(8,128)(2,1)} %copy-done.1) | copy-start | bytes 2359300
  180.3 12.7 %copy-start.4 = (bf16[384,1024]{0,1:T(8,128)(2,1)S(1)}, bf16[384,1024]{0,1:T(8,128)(2,1)}, u32[]{:S(2)}) copy-start(bf16[384,1024]{0,1:T(8,128)(2,1)} %copy-done.3) | copy-start | bytes 2359300
  193.2 14.6 %copy-start.14 = (f32[8,4,128,64]{2,3,1,0:T(8,128)S(1)}, f32[8,4,128,64]{2,3,1,0:T(8,128)}, u32[]{:S(2)}) copy-start(f32[8,4,128,64]{2,3,1,0:T(8,128)} %custom-call.1) | copy-start | bytes 3145732
  364.3 8.9 %copy-start.16 = (f32[2880]{0:T(1024)S(1)}, f32[2880]{0:T(1024)}, u32[]{:S(2)}) copy-start(f32[2880]{0:T(1024)} %param.21) | copy-start | bytes 34564
  613.4 12.4 %copy-start.15 = (s32[1,128,4]{1,2,0:T(4,128)S(1)}, s32[1,128,4]{1,2,0:T(4,128)}, u32[]{:S(2)}) copy-start(s32[1,128,4]{1,2,0:T(4,128)} %param.23) | copy-start | bytes 6148
  613.4 170.3 %all-to-all-start.1 = ((bf16[128,10,2880]{2,1,0:T(8,128)(2,1)}), bf16[128,10,2880]{2,1,0:T(8,128)(2,1)}, u32[]{:S(2)}, u32[]{:S(2)}) async-start(bf16[128,10,2880]{2,1,0:T(8,128)(2,1)} %reshape.321), calls=%async_computation.1 | async-start | bytes 24117248 | tf_op jit(solution)/shard_map/all_to_all | solution.py:161
  (2 other events, 6.0 us)
Sparse Core Ops, SparseCore 0:
  128.6 123.5 all-gather.1
